TPU v7x, 256 devices: a whole 4x4x8 slice. The times are simulated.
256 devices in a mesh: dp: 8 (over y, core), seq: 32 (over x, z).
Axes of the slice: x: 4, y: 4, z: 8, core: 2. Of those that a mesh axis runs over, the one named last changes fastest.
Arguments:
- queries: bfloat16 [16, 2048, 1536], P('dp', 'seq'), may hold values from -6 to 6
- key_rows: bfloat16 [16, 2048, 1536], P('dp', 'seq'), may hold values from -6 to 6
- value_rows: bfloat16 [16, 2048, 1536], P('dp', 'seq'), may hold values from -6 to 6
- layer_input: bfloat16 [16, 2048, 1536], P('dp', 'seq'), may hold values from -6 to 6
- utt_lengths: int32 [16], P('dp'), may hold values from 512 to 2048, as said below
- out_weight: bfloat16 [1536, 1536], replicated, may hold values from -0.15625 to 0.15625
- conv_kernel: bfloat16 [31, 1536], replicated, may hold values from -1 to 1
- conv_cotangent: bfloat16 [16, 2048, 1536], P('dp', 'seq'), may hold values from -6 to 6
- pick_weight: int32 [23592], replicated, may hold values from 0 to 2359295
- pick_kernel: int32 [476], replicated, may hold values from 0 to 47615
Outputs:
- conv_out: bfloat16 [16, 2048, 1536], P('dp', 'seq')
- context_grad: bfloat16 [16, 2048, 1536], P('dp', 'seq')
- weight_picks: float32 [23592], replicated
- kernel_picks: float32 [476], replicated
Inputs may be any that keep to these rules, and one draw needn't show every extreme that they name: `utt_lengths`: the first utterance fills all 2048 slots and the last has 512 valid frames.
All inputs are finite; a program needn't handle non-finite values.
Results may differ from a plain program's by a relative error of at most 0.0056.
Values may be sent and summed in bfloat16 or wider, within the bound.
No kernel may reach another device: no remote copies, remote signals or barrier semaphores. Data moves between devices by JAX's collectives and lax.ppermute only.
A program may use at most 128 MiB of HBM per device.

v0:
```python
import math
import jax
import jax.numpy as jnp
from jax import lax
from jax.sharding import PartitionSpec as P

HEADS = 16
neg_big = -1e30


def padded(value, sides, width):
    for axis, dim in sides:
        count, length = (lax.axis_size(axis), value.shape[dim])
        up = [(i, (i + 1) % count) for i in range(count - 1)]
        down = [(j, i) for i, j in up]
        last = lax.slice_in_dim(value, length - width, length, axis=dim)
        leading = lax.slice_in_dim(value, 0, width, axis=dim)
        before = lax.ppermute(last, axis, up)
        after = lax.ppermute(leading, axis, down)
        value = jnp.concatenate([before, value, after], axis=dim)
    return value


def softmax_rows(scores, key_ok):
    scores = jnp.where(key_ok, scores, neg_big)
    row_max = jnp.max(scores, axis=-1, keepdims=True)
    probs = jnp.exp(scores - row_max)
    return (probs.astype(jnp.bfloat16), jnp.sum(probs, axis=-1))


def pick_entries(table, picks):
    flat = table.reshape(-1)
    lane = math.gcd(flat.shape[0], 128)
    blocks = flat.reshape(flat.shape[0] // lane, lane)
    chosen = jnp.take(blocks, picks // lane, axis=0)
    lane_ids = jnp.arange(lane, dtype=jnp.int32)
    hit = lane_ids[None, :] == (picks % lane)[:, None]
    return jnp.sum(jnp.where(hit, chosen, jnp.float32(0.0)), axis=1)


def on_device(
    queries,
    key_rows,
    value_rows,
    layer_input,
    utt_lengths,
    out_weight,
    conv_kernel,
    conv_cotangent,
    pick_weight,
    pick_kernel,
):
    local_utts, frames_dev, width = queries.shape
    seq_count = lax.axis_size("seq")
    full_frames = frames_dev * seq_count
    head_size = width // HEADS
    score_scale = 1.0 / math.sqrt(head_size)
    first_frame = lax.axis_index("seq") * frames_dev
    local_ids = first_frame + jnp.arange(frames_dev, dtype=jnp.int32)
    valid_rows = (local_ids[None, :] < utt_lengths[:, None]).astype(jnp.float32)
    all_keys, all_values = (
        lax.all_gather(key_rows, "seq", axis=1, tiled=True),
        lax.all_gather(value_rows, "seq", axis=1, tiled=True),
    )
    full_ids = jnp.arange(full_frames, dtype=jnp.int32)

    def one_utt(item):
        query_utt, key_utt, value_utt, length_utt = item
        query_heads = query_utt.reshape(frames_dev, HEADS, head_size)
        key_heads = key_utt.reshape(full_frames, HEADS, head_size)
        value_heads = value_utt.reshape(full_frames, HEADS, head_size)
        scores = (
            jnp.einsum("qhd,khd->hqk", query_heads, key_heads, preferred_element_type=jnp.float32)
            * score_scale
        )
        weights, denom = softmax_rows(scores, (full_ids < length_utt)[None, None, :])
        out_rows = jnp.einsum(
            "hqk,khd->qhd", weights, value_heads, preferred_element_type=jnp.float32
        )
        out_rows = out_rows / denom.transpose(1, 0)[:, :, None]
        return out_rows.astype(jnp.bfloat16).reshape(frames_dev, width)

    context = lax.map(one_utt, (queries, all_keys, all_values, utt_lengths))
    context_flat = context.reshape(local_utts * frames_dev, width)
    projected = jnp.dot(context_flat, out_weight, preferred_element_type=jnp.float32).reshape(
        local_utts, frames_dev, width
    )
    hidden = ((layer_input.astype(jnp.float32) + projected) * valid_rows[:, :, None]).astype(
        jnp.bfloat16
    )
    tap_count = conv_kernel.shape[0]
    half_taps = (tap_count - 1) // 2
    kernel_f = conv_kernel.astype(jnp.float32)
    hidden_pad = padded(hidden, (("seq", 1),), half_taps)
    cot_f = conv_cotangent.astype(jnp.float32)
    conv_sum = jnp.zeros((local_utts, frames_dev, width), jnp.float32)
    kernel_rows = []
    for offset in range(tap_count):
        window = hidden_pad[:, offset : offset + frames_dev].astype(jnp.float32)
        conv_sum = conv_sum + kernel_f[offset] * window
        kernel_rows.append(jnp.sum(window * cot_f, axis=(0, 1)))
    conv_out = conv_sum.astype(jnp.bfloat16)
    kernel_grad = jnp.stack(kernel_rows)
    cot_pad = padded(conv_cotangent, (("seq", 1),), half_taps).astype(jnp.float32)
    back_sum = jnp.zeros((local_utts, frames_dev, width), jnp.float32)
    for offset in range(tap_count):
        begin = 2 * half_taps - offset
        back_sum = back_sum + kernel_f[offset] * cot_pad[:, begin : begin + frames_dev]
    hidden_grad = (back_sum * valid_rows[:, :, None]).astype(jnp.bfloat16)
    grad_flat = hidden_grad.reshape(local_utts * frames_dev, width)
    weight_grad = lax.dot_general(
        context_flat, grad_flat, (((0,), (0,)), ((), ())), preferred_element_type=jnp.float32
    )
    context_grad = lax.dot_general(
        grad_flat, out_weight, (((1,), (1,)), ((), ())), preferred_element_type=jnp.float32
    )
    context_grad = context_grad.reshape(local_utts, frames_dev, width).astype(jnp.bfloat16)
    weight_vals = pick_entries(weight_grad, pick_weight)
    kernel_vals = pick_entries(kernel_grad, pick_kernel)
    weight_sum, kernel_sum = lax.psum((weight_vals, kernel_vals), ("dp", "seq"))
    total_slots = local_utts * lax.axis_size("dp") * full_frames
    norm_factor = 1.0 / math.sqrt(total_slots)
    return (conv_out, context_grad, weight_sum * norm_factor, kernel_sum * norm_factor)


def solution(mesh):
    placed = (
        P("dp", "seq", None),
        P("dp", "seq", None),
        P("dp", "seq", None),
        P("dp", "seq", None),
        P("dp"),
        P(),
        P(),
        P("dp", "seq", None),
        P(),
        P(),
    )
    return jax.shard_map(
        on_device,
        mesh=mesh,
        in_specs=placed,
        out_specs=(P("dp", "seq", None), P("dp", "seq", None), P(), P()),
        check_vma=False,
    )
```

profile of v0, /device:TPU:1, one launch (start us, length us, event | category | flops | bytes accessed | tf_op | source)
XLA Modules:
  0.0 756.6 jit_solution(8033392045944065864)
XLA Ops:
  7.2 2.1 copy.22
  9.4 2.2 copy.23
  11.7 1.0 fusion.165
  12.6 4.4 collective-permute-start.2
  17.0 1.3 collective-permute-start.3
  18.3 0.9 convert_element_type.130
  20.1 0.7 compare_convert_fusion
  20.8 1.3 add_select_fusion.3
  22.1 1.3 compare_and_fusion.1
  23.4 1.6 compare_and_fusion
  25.0 1.6 add_select_fusion.1
  26.6 0.6 pad_clamp_fusion.1
  27.2 1.3 maximum_convert_fusion
  28.5 3.3 fusion.104
  32.1 2.4 fusion.34
  34.5 99.7 %all-gather.3.cloned.1.call-done = bf16[2,2048,1536]{2,0,1:T(2,128)(2,1)} async-done(((bf16[2,64,1536]{2,0,1:T(2,128)(2,1)}), bf16[2,2048,1536]{2,0,1:T(2,128)(2,1)}) %all-gather.3.cloned.1.call-update) | async-done | bytes 12582928 | tf_op jit(solution)/shard_map/all_gather | solution.py:63
  134.2 31.1 %copy.24 = bf16[2,2048,1536]{1,2,0:T(8,128)(2,1)} copy(bf16[2,2048,1536]{2,0,1:T(2,128)(2,1)} %all-gather.3.cloned.1.call-done) | data formatting | bytes 25165824
  165.4 88.2 %all-gather.5.cloned.1.call-done = bf16[2,2048,1536]{2,0,1:T(2,128)(2,1)} async-done(((bf16[2,64,1536]{2,0,1:T(2,128)(2,1)}), bf16[2,2048,1536]{2,0,1:T(2,128)(2,1)}) %all-gather.5.cloned.1.call-update) | async-done | bytes 12582928 | tf_op jit(solution)/shard_map/all_gather | solution.py:62
  253.6 31.1 %copy.25 = bf16[2,2048,1536]{1,2,0:T(8,128)(2,1)} copy(bf16[2,2048,1536]{2,0,1:T(2,128)(2,1)} %all-gather.5.cloned.1.call-done) | data formatting | bytes 25165824
  284.7 51.8 %while.11 = (s32[]{:T(128)}, bf16[2,64,1536]{2,1,0:T(8,128)(2,1)S(1)}, bf16[2,2048,1536]{1,2,0:T(8,128)(2,1)}, s32[2]{0:T(128)S(1)}, bf16[2,64,1536]{2,1,0:T(8,1...) while((s32[]{:T(128)}, bf16[2,64,1536]{2,1,0:T(8,128)(2,1)S(1)}, ...), condition=%wide.region_3.4_spmd.clone, body=%wide.region_0.3_spmd.clone.sunk | while | flops 828571648 | bytes 65302632 | solution.py:83
  284.7 11.9 %constant_dynamic-slice_fusion.5 = (bf16[1,2048,1536]{1,2,0:T(8,128)(2,1)}, bf16[1,2048,1536]{1,2,0:T(8,128)(2,1)}) fusion(bf16[2,2048,1536]{1,2,0:T(8,128)(2,1)} %get-tuple-element.212, s32[]{:T(128)} %get-tuple-element.200, bf16[2,2048,1536]{1,2,0:T(8,128)(2,1)} %get-tuple-element.209), kind=kLoop, calls=%fused_computation.20.clone.1 | loop fusion | bytes 25165828 | tf_op jit(solution)/shard_map/while/body/jit(dynamic_index_in_dim)/dynamic_slice | solution.py:83
  296.7 0.6 dynamic_slice.27
  297.2 0.7 iota_compare_fusion.4
  298.2 5.0 fusion.182
  303.2 1.9 fusion.183
  305.1 5.1 fusion.184
  310.6 11.9 %constant_dynamic-slice_fusion.5 = (bf16[1,2048,1536]{1,2,0:T(8,128)(2,1)}, bf16[1,2048,1536]{1,2,0:T(8,128)(2,1)}) fusion(bf16[2,2048,1536]{1,2,0:T(8,128)(2,1)} %get-tuple-element.212, s32[]{:T(128)} %get-tuple-element.200, bf16[2,2048,1536]{1,2,0:T(8,128)(2,1)} %get-tuple-element.209), kind=kLoop, calls=%fused_computation.20.clone.1 | loop fusion | bytes 25165828 | tf_op jit(solution)/shard_map/while/body/jit(dynamic_index_in_dim)/dynamic_slice | solution.py:83
  322.6 0.6 dynamic_slice.27
  323.2 0.7 iota_compare_fusion.4
  324.1 5.0 fusion.182
  329.1 1.9 fusion.183
  331.0 5.1 fusion.184
  336.6 5.0 convolution_bitcast_fusion
  341.6 0.8 fusion.37
  342.4 10.5 %reshape_reshape.6 = f32[18432,128]{1,0:T(8,128)} reshape(f32[1536,1536]{1,0:T(8,128)} %convolution_bitcast_fusion) | data formatting | bytes 18874368 | tf_op jit(solution)/shard_map/reshape;reshape | solution.py:34
  353.0 48.0 %gather_fusion = f32[23592,128]{1,0:T(8,128)} fusion(f32[18432,128]{1,0:T(8,128)} %reshape_reshape.6, s32[24576]{0:T(1024)S(1)} %pad_clamp_fusion), kind=kCustom, calls=%fused_computation | custom fusion | bytes 24252576 | tf_op jit(solution)/shard_map/jit(_take)/gather | solution.py:35
  401.3 22.9 %select_reduce_fusion = f32[23592]{0:T(1024)} fusion(f32[23592,128]{1,0:T(8,128)} %gather_fusion, s32[23592]{0:T(1024)S(1)} %copy-done.2, pred[23592]{0:T(1024)(128)(4,1)S(1)} %copy-done.4), kind=kLoop, calls=%fused_computation.25 | loop fusion | flops 12055512 | bytes 12291432 | tf_op jit(solution)/shard_map/reduce_sum | solution.py:38
  424.3 1.4 collective-permute-start
  425.7 1.3 collective-permute-start.1
  427.0 235.6 %all-reduce.2.cloned.1.call-done = f32[23592]{0:T(1024)} async-done(((f32[23592]{0:T(1024)}), f32[23592]{0:T(1024)}) %all-reduce.2.cloned.1.call-update) | async-done | bytes 94384 | tf_op jit(solution)/shard_map/psum | solution.py:120
  662.5 1.5 broadcast_multiply_fusion
  664.1 1.2 fusion.85
  665.4 1.3 fusion.101
  666.9 0.8 fusion.100
  667.9 0.8 fusion.84
  669.1 1.2 gather_fusion.1
  670.6 74.1 %psum.15 = f32[476]{0:T(512)S(1)} all-reduce(f32[476]{0:T(512)S(1)} %select_reduce_fusion.1), channel_id=1, replica_groups=mesh['dp'=8,'seq'=32] {'dp','seq'}, use_global_device_ids=true, to_apply=%region_38.39 | all-reduce | flops 476 | bytes 3808 | tf_op jit(solution)/shard_map/psum | solution.py:120
  745.6 4.5 fusion.70
  (213 shorter events, 3.9 us)
Async XLA Ops:
  7.2 127.1 %all-gather.3.cloned.1.call-start = ((), (), s32[]{:S(2)}) async-start(), calls=%async_computation | async-start | bytes 12976128 | tf_op jit(solution)/shard_map/all_gather | solution.py:63
  9.4 244.2 %all-gather.5.cloned.1.call-start = ((), (), s32[]{:S(2)}) async-start(), calls=%async_computation.1 | async-start | bytes 12976128 | tf_op jit(solution)/shard_map/all_gather | solution.py:62
  11.6 650.9 %all-reduce.2.cloned.1.call-start = ((), (), s32[]{:S(2)}) async-start(), calls=%async_computation.2 | async-start | bytes 196608 | tf_op jit(solution)/shard_map/psum | solution.py:120
  12.6 14.5 %collective-permute-start.2 = (bf16[2,15,1536]{2,1,0:T(8,128)(2,1)S(1)}, bf16[2,15,1536]{2,1,0:T(8,128)(2,1)S(1)}, u32[]{:S(2)}, u32[]{:S(2)}) collective-permute-start(bf16[2,15,1536]{2,1,0:T(8,128)(2,1)S(1)} %get-tuple-element.144), channel_id=1, source_target_pairs={{0,1},{1,2},{2,3},{3,4},{4,5},{5,6},{6,7},{7,8},{8,9},{9,10},{10,1... | collective-permute-start | bytes 276488 | tf_op jit(solution)/shard_map/ppermute | solution.py:18
  17.0 10.1 %collective-permute-start.3 = (bf16[2,15,1536]{2,1,0:T(8,128)(2,1)S(1)}, bf16[2,15,1536]{2,1,0:T(8,128)(2,1)S(1)}, u32[]{:S(2)}, u32[]{:S(2)}) collective-permute-start(bf16[2,15,1536]{2,1,0:T(8,128)(2,1)S(1)} %get-tuple-element.145), channel_id=1, source_target_pairs={{1,0},{2,1},{3,2},{4,3},{5,4},{6,5},{7,6},{8,7},{9,8},{10,9},{11,1... | collective-permute-start | bytes 276488 | tf_op jit(solution)/shard_map/ppermute | solution.py:19
  19.5 12.3 %copy-start.43 = (f32[1536]{0:T(1024)}, f32[1536]{0:T(1024)S(1)}, u32[]{:S(2)}) copy-start(f32[1536]{0:T(1024)S(1)} %get-tuple-element.112) | copy-start | bytes 18436
  19.5 12.3 %copy-start.45 = (f32[1536]{0:T(1024)}, f32[1536]{0:T(1024)S(1)}, u32[]{:S(2)}) copy-start(f32[1536]{0:T(1024)S(1)} %get-tuple-element.113) | copy-start | bytes 18436
  165.4 119.3 %copy-start.1 = (bf16[2,64,1536]{2,1,0:T(8,128)(2,1)S(1)}, bf16[2,64,1536]{2,1,0:T(8,128)(2,1)}, u32[]{:S(2)}) copy-start(bf16[2,64,1536]{2,1,0:T(8,128)(2,1)} %param.12) | copy-start | bytes 1179652
  165.4 119.3 %copy-start.70 = (s32[2]{0:T(128)S(1)}, s32[2]{0:T(128)}, u32[]{:S(2)}) copy-start(s32[2]{0:T(128)} %param.16) | copy-start | bytes 28
  353.0 48.0 %copy-start.2 = (s32[23592]{0:T(1024)S(1)}, s32[23592]{0:T(1024)}, u32[]{:S(2)}) copy-start(s32[23592]{0:T(1024)} %add_select_fusion.1) | copy-start | bytes 283108
  353.0 48.0 %copy-start.4 = (pred[23592]{0:T(1024)(128)(4,1)S(1)}, pred[23592]{0:T(1024)(128)(4,1)}, u32[]{:S(2)}) copy-start(pred[23592]{0:T(1024)(128)(4,1)} %get-tuple-element.138) | copy-start | bytes 70780
  400.9 263.2 %copy-start = (bf16[2,64,1536]{2,1,0:T(8,128)(2,1)S(1)}, bf16[2,64,1536]{2,1,0:T(8,128)(2,1)}, u32[]{:S(2)}) copy-start(bf16[2,64,1536]{2,1,0:T(8,128)(2,1)} %param.19) | copy-start | bytes 1179652
  400.9 268.2 %copy-start.67 = (s32[1024]{0:T(1024)S(1)}, s32[1024]{0:T(1024)}, u32[]{:S(2)}) copy-start(s32[1024]{0:T(1024)} %pad_clamp_fusion.1) | copy-start | bytes 12292
  401.0 269.3 %copy-start.68 = (s32[476]{0:T(512)S(1)}, s32[476]{0:T(512)}, u32[]{:S(2)}) copy-start(s32[476]{0:T(512)} %add_select_fusion.3) | copy-start | bytes 5716
  401.0 269.3 %copy-start.69 = (pred[476]{0:T(512)(128)(4,1)S(1)}, pred[476]{0:T(512)(128)(4,1)}, u32[]{:S(2)}) copy-start(pred[476]{0:T(512)(128)(4,1)} %get-tuple-element.136) | copy-start | bytes 1432
  401.0 344.3 %copy-start.6 = (f32[1536]{0:T(1024)S(1)}, f32[1536]{0:T(1024)}, u32[]{:S(2)}) copy-start(f32[1536]{0:T(1024)} %copy-done.5) | copy-start | bytes 18436
  401.0 344.3 %copy-start.8 = (f32[1536]{0:T(1024)S(1)}, f32[1536]{0:T(1024)}, u32[]{:S(2)}) copy-start(f32[1536]{0:T(1024)} %copy-done.7) | copy-start | bytes 18436
  401.0 344.3 %copy-start.10 = (f32[1536]{0:T(1024)S(1)}, f32[1536]{0:T(1024)}, u32[]{:S(2)}) copy-start(f32[1536]{0:T(1024)} %copy-done.9) | copy-start | bytes 18436
  401.0 344.3 %copy-start.12 = (f32[1536]{0:T(1024)S(1)}, f32[1536]{0:T(1024)}, u32[]{:S(2)}) copy-start(f32[1536]{0:T(1024)} %copy-done.11) | copy-start | bytes 18436
  401.0 344.3 %copy-start.14 = (f32[1536]{0:T(1024)S(1)}, f32[1536]{0:T(1024)}, u32[]{:S(2)}) copy-start(f32[1536]{0:T(1024)} %copy-done.13) | copy-start | bytes 18436
  401.0 344.3 %copy-start.16 = (f32[1536]{0:T(1024)S(1)}, f32[1536]{0:T(1024)}, u32[]{:S(2)}) copy-start(f32[1536]{0:T(1024)} %copy-done.15) | copy-start | bytes 18436
  401.0 344.3 %copy-start.18 = (f32[1536]{0:T(1024)S(1)}, f32[1536]{0:T(1024)}, u32[]{:S(2)}) copy-start(f32[1536]{0:T(1024)} %copy-done.17) | copy-start | bytes 18436
  401.0 344.3 %copy-start.20 = (f32[1536]{0:T(1024)S(1)}, f32[1536]{0:T(1024)}, u32[]{:S(2)}) copy-start(f32[1536]{0:T(1024)} %copy-done.19) | copy-start | bytes 18436
  401.1 344.3 %copy-start.22 = (f32[1536]{0:T(1024)S(1)}, f32[1536]{0:T(1024)}, u32[]{:S(2)}) copy-start(f32[1536]{0:T(1024)} %copy-done.21) | copy-start | bytes 18436
  401.1 344.3 %copy-start.24 = (f32[1536]{0:T(1024)S(1)}, f32[1536]{0:T(1024)}, u32[]{:S(2)}) copy-start(f32[1536]{0:T(1024)} %copy-done.23) | copy-start | bytes 18436
  401.1 344.3 %copy-start.26 = (f32[1536]{0:T(1024)S(1)}, f32[1536]{0:T(1024)}, u32[]{:S(2)}) copy-start(f32[1536]{0:T(1024)} %copy-done.25) | copy-start | bytes 18436
  401.1 344.3 %copy-start.28 = (f32[1536]{0:T(1024)S(1)}, f32[1536]{0:T(1024)}, u32[]{:S(2)}) copy-start(f32[1536]{0:T(1024)} %copy-done.27) | copy-start | bytes 18436
  401.1 344.3 %copy-start.30 = (f32[1536]{0:T(1024)S(1)}, f32[1536]{0:T(1024)}, u32[]{:S(2)}) copy-start(f32[1536]{0:T(1024)} %copy-done.29) | copy-start | bytes 18436
  401.1 344.3 %copy-start.32 = (f32[1536]{0:T(1024)S(1)}, f32[1536]{0:T(1024)}, u32[]{:S(2)}) copy-start(f32[1536]{0:T(1024)} %copy-done.31) | copy-start | bytes 18436
  401.1 344.3 %copy-start.34 = (f32[1536]{0:T(1024)S(1)}, f32[1536]{0:T(1024)}, u32[]{:S(2)}) copy-start(f32[1536]{0:T(1024)} %copy-done.33) | copy-start | bytes 18436
  401.1 344.3 %copy-start.36 = (f32[1536]{0:T(1024)S(1)}, f32[1536]{0:T(1024)}, u32[]{:S(2)}) copy-start(f32[1536]{0:T(1024)} %copy-done.35) | copy-start | bytes 18436
  401.1 344.3 %copy-start.38 = (f32[1536]{0:T(1024)S(1)}, f32[1536]{0:T(1024)}, u32[]{:S(2)}) copy-start(f32[1536]{0:T(1024)} %copy-done.37) | copy-start | bytes 18436
  401.1 344.3 %copy-start.40 = (f32[1536]{0:T(1024)S(1)}, f32[1536]{0:T(1024)}, u32[]{:S(2)}) copy-start(f32[1536]{0:T(1024)} %copy-done.39) | copy-start | bytes 18436
  401.2 344.3 %copy-start.42 = (f32[1536]{0:T(1024)S(1)}, f32[1536]{0:T(1024)}, u32[]{:S(2)}) copy-start(f32[1536]{0:T(1024)} %copy-done.41) | copy-start | bytes 18436
  401.2 344.3 %copy-start.44 = (f32[1536]{0:T(1024)S(1)}, f32[1536]{0:T(1024)}, u32[]{:S(2)}) copy-start(f32[1536]{0:T(1024)} %copy-done.43) | copy-start | bytes 18436
  401.2 344.3 %copy-start.46 = (f32[1536]{0:T(1024)S(1)}, f32[1536]{0:T(1024)}, u32[]{:S(2)}) copy-start(f32[1536]{0:T(1024)} %copy-done.45) | copy-start | bytes 18436
  401.2 344.3 %copy-start.48 = (f32[1536]{0:T(1024)S(1)}, f32[1536]{0:T(1024)}, u32[]{:S(2)}) copy-start(f32[1536]{0:T(1024)} %copy-done.47) | copy-start | bytes 18436
  401.2 344.3 %copy-start.50 = (f32[1536]{0:T(1024)S(1)}, f32[1536]{0:T(1024)}, u32[]{:S(2)}) copy-start(f32[1536]{0:T(1024)} %copy-done.49) | copy-start | bytes 18436
  401.2 344.3 %copy-start.52 = (f32[1536]{0:T(1024)S(1)}, f32[1536]{0:T(1024)}, u32[]{:S(2)}) copy-start(f32[1536]{0:T(1024)} %copy-done.51) | copy-start | bytes 18436
  401.2 344.3 %copy-start.54 = (f32[1536]{0:T(1024)S(1)}, f32[1536]{0:T(1024)}, u32[]{:S(2)}) copy-start(f32[1536]{0:T(1024)} %copy-done.53) | copy-start | bytes 18436
  401.2 344.3 %copy-start.56 = (f32[1536]{0:T(1024)S(1)}, f32[1536]{0:T(1024)}, u32[]{:S(2)}) copy-start(f32[1536]{0:T(1024)} %copy-done.55) | copy-start | bytes 18436
  401.2 344.3 %copy-start.58 = (f32[1536]{0:T(1024)S(1)}, f32[1536]{0:T(1024)}, u32[]{:S(2)}) copy-start(f32[1536]{0:T(1024)} %copy-done.57) | copy-start | bytes 18436
  401.2 344.3 %copy-start.60 = (f32[1536]{0:T(1024)S(1)}, f32[1536]{0:T(1024)}, u32[]{:S(2)}) copy-start(f32[1536]{0:T(1024)} %copy-done.59) | copy-start | bytes 18436
  401.3 344.3 %copy-start.62 = (f32[1536]{0:T(1024)S(1)}, f32[1536]{0:T(1024)}, u32[]{:S(2)}) copy-start(f32[1536]{0:T(1024)} %copy-done.61) | copy-start | bytes 18436
  401.3 344.3 %copy-start.64 = (f32[1536]{0:T(1024)S(1)}, f32[1536]{0:T(1024)}, u32[]{:S(2)}) copy-start(f32[1536]{0:T(1024)} %copy-done.63) | copy-start | bytes 18436
  401.3 344.3 %copy-start.66 = (f32[1536]{0:T(1024)S(1)}, f32[1536]{0:T(1024)}, u32[]{:S(2)}) copy-start(f32[1536]{0:T(1024)} %copy-done.65) | copy-start | bytes 18436
  424.3 239.8 %collective-permute-start = (bf16[2,15,1536]{2,1,0:T(8,128)(2,1)S(1)}, bf16[2,15,1536]{2,1,0:T(8,128)(2,1)S(1)}, u32[]{:S(2)}, u32[]{:S(2)}) collective-permute-start(bf16[2,15,1536]{2,1,0:T(8,128)(2,1)S(1)} %get-tuple-element.146), channel_id=1, source_target_pairs={{0,1},{1,2},{2,3},{3,4},{4,5},{5,6},{6,7},{7,8},{8,9},{9,10},{10,1... | collective-permute-start | bytes 276488 | tf_op jit(solution)/shard_map/ppermute | solution.py:18
  425.7 239.7 %collective-permute-start.1 = (bf16[2,15,1536]{2,1,0:T(8,128)(2,1)S(1)}, bf16[2,15,1536]{2,1,0:T(8,128)(2,1)S(1)}, u32[]{:S(2)}, u32[]{:S(2)}) collective-permute-start(bf16[2,15,1536]{2,1,0:T(8,128)(2,1)S(1)} %get-tuple-element.147), channel_id=1, source_target_pairs={{1,0},{2,1},{3,2},{4,3},{5,4},{6,5},{7,6},{8,7},{9,8},{10,9},{11,1... | collective-permute-start | bytes 276488 | tf_op jit(solution)/shard_map/ppermute | solution.py:19
  (34 other events, 375.5 us)
Sparse Core Ops, SparseCore 0:
  11.2 123.0 all-gather.2
  136.8 116.7 all-gather.4
  424.3 238.1 all-reduce.1
where the time goes:
time: 759 us; the launch traced here: 757 us
  waiting for transfers between devices  424 us (56%)
  local copies, waits for them, and re-layouts  155 us (20%)
  blocking collectives  74.1 us (10%)
  other arithmetic  51.7 us (7%)
  matrix products  28.4 us (4%)
  between operations  15.2 us (2%)
  starting transfers between devices  8.5 us (1%)
    psum x1, waiting for transfers between devices, on_device(): weight_sum, kernel_sum = lax.psum((weight_vals, kernel_vals), ('dp', 'seq'))  236 us
    all_gather x1, waiting for transfers between devices, on_device(): lax.all_gather(value_rows, 'seq', axis=1, tiled=True)  99.7 us
    all_gather x1, waiting for transfers between devices, on_device(): lax.all_gather(key_rows, 'seq', axis=1, tiled=True)  88.2 us
    psum x1, blocking collectives, on_device(): weight_sum, kernel_sum = lax.psum((weight_vals, kernel_vals), ('dp', 'seq'))  74.1 us
    unnamed x154, local copies, waits for them, and re-layouts  66.9 us
    gather x2, local copies, waits for them, and re-layouts, pick_entries(): chosen = jnp.take(blocks, picks // lane, axis=0)  49.1 us
    dynamic_slice x6, local copies, waits for them, and re-layouts, on_device(): context = lax.map(one_utt, (queries, all_keys, all_values, utt_lengths))  25.1 us
    reduce_sum x2, other arithmetic, pick_entries(): return jnp.sum(jnp.where(hit, chosen, jnp.float32(0.0)), axis=1)  23.2 us
  transfers between devices with their start and end apart: 7, of which 3 were waited for; matrix products, arithmetic and copies ran while one was open for 7% of the time, Pallas kernels for 0%

commit v1 on v0

--- a/solution.py
+++ b/solution.py
@@ -117,7 +117,7 @@
     context_grad = context_grad.reshape(local_utts, frames_dev, width).astype(jnp.bfloat16)
     weight_vals = pick_entries(weight_grad, pick_weight)
     kernel_vals = pick_entries(kernel_grad, pick_kernel)
-    weight_sum, kernel_sum = lax.psum((weight_vals, kernel_vals), ("dp", "seq"))
+    weight_sum, kernel_sum = lax.psum(lax.psum((weight_vals, kernel_vals), "seq"), "dp")
     total_slots = local_utts * lax.axis_size("dp") * full_frames
     norm_factor = 1.0 / math.sqrt(total_slots)
     return (conv_out, context_grad, weight_sum * norm_factor, kernel_sum * norm_factor)

time: 759 us -> 642 us (0.85)
  waiting for transfers between devices: 424 us -> 292 us
  blocking collectives: 74.1 us -> 87.2 us
    psum x1 -> x2, waiting for transfers between devices: 236 us -> 104 us  [the longest x1 64.2 us: on_device(): lax.psum(lax.psum((weight_vals, kernel_vals), 'seq'), 'dp')]
    psum x1 -> x2, blocking collectives: 74.1 us -> 87.2 us  [the longest x1 60.1 us: on_device(): lax.psum((weight_vals, kernel_vals), 'seq')]
  transfers between devices with their start and end apart: 7 -> 8, of which waited for: 3 -> 4; matrix products, arithmetic and copies ran while one was open for 7% -> 22% of each run, Pallas kernels for 0% -> 0%
where the time goes in v1:
time: 642 us; the launch traced here: 638 us
  waiting for transfers between devices  292 us (45%)
  local copies, waits for them, and re-layouts  155 us (24%)
  blocking collectives  87.2 us (14%)
  other arithmetic  51.7 us (8%)
  matrix products  28.3 us (4%)
  between operations  15.3 us (2%)
  starting transfers between devices  8.79 us (1%)
    all_gather x1, waiting for transfers between devices, on_device(): lax.all_gather(value_rows, 'seq', axis=1, tiled=True)  99.7 us
    all_gather x1, waiting for transfers between devices, on_device(): lax.all_gather(key_rows, 'seq', axis=1, tiled=True)  88.2 us
    unnamed x154, local copies, waits for them, and re-layouts  66.9 us
    psum x1, waiting for transfers between devices, on_device(): lax.psum(lax.psum((weight_vals, kernel_vals), 'seq'), 'dp')  64.2 us
    psum x1, blocking collectives, on_device(): lax.psum((weight_vals, kernel_vals), 'seq')  60.1 us
    gather x2, local copies, waits for them, and re-layouts, pick_entries(): chosen = jnp.take(blocks, picks // lane, axis=0)  49.1 us
    psum x1, waiting for transfers between devices, on_device(): lax.psum((weight_vals, kernel_vals), 'seq')  39.8 us
    psum x1, blocking collectives, on_device(): lax.psum(lax.psum((weight_vals, kernel_vals), 'seq'), 'dp')  27.1 us
  transfers between devices with their start and end apart: 8, of which 4 were waited for; matrix products, arithmetic and copies ran while one was open for 22% of the time, Pallas kernels for 0%

profile of v1, /device:TPU:1, one launch (start us, length us, event | category | flops | bytes accessed | tf_op | source)
XLA Modules:
  0.0 638.4 jit_solution(8083633150296259476)
XLA Ops:
  7.2 2.1 copy.22
  9.4 2.2 copy.23
  11.7 1.0 fusion.165
  12.6 4.4 collective-permute-start.2
  17.0 1.3 collective-permute-start.3
  18.3 0.9 convert_element_type.130
  20.1 0.7 compare_convert_fusion
  20.8 1.3 add_select_fusion.3
  22.1 1.3 compare_and_fusion.1
  23.4 1.6 compare_and_fusion
  25.0 1.6 add_select_fusion.1
  26.5 0.6 pad_clamp_fusion.1
  27.1 1.3 maximum_convert_fusion
  28.5 3.3 fusion.104
  32.1 2.4 fusion.34
  34.5 99.7 %all-gather.3.cloned.1.call-done = bf16[2,2048,1536]{2,0,1:T(2,128)(2,1)} async-done(((bf16[2,64,1536]{2,0,1:T(2,128)(2,1)}), bf16[2,2048,1536]{2,0,1:T(2,128)(2,1)}) %all-gather.3.cloned.1.call-update) | async-done | bytes 12582928 | tf_op jit(solution)/shard_map/all_gather | solution.py:63
  134.2 31.1 %copy.24 = bf16[2,2048,1536]{1,2,0:T(8,128)(2,1)} copy(bf16[2,2048,1536]{2,0,1:T(2,128)(2,1)} %all-gather.3.cloned.1.call-done) | data formatting | bytes 25165824
  165.4 88.2 %all-gather.5.cloned.1.call-done = bf16[2,2048,1536]{2,0,1:T(2,128)(2,1)} async-done(((bf16[2,64,1536]{2,0,1:T(2,128)(2,1)}), bf16[2,2048,1536]{2,0,1:T(2,128)(2,1)}) %all-gather.5.cloned.1.call-update) | async-done | bytes 12582928 | tf_op jit(solution)/shard_map/all_gather | solution.py:62
  253.6 31.1 %copy.25 = bf16[2,2048,1536]{1,2,0:T(8,128)(2,1)} copy(bf16[2,2048,1536]{2,0,1:T(2,128)(2,1)} %all-gather.5.cloned.1.call-done) | data formatting | bytes 25165824
  284.7 51.8 %while.11 = (s32[]{:T(128)}, bf16[2,64,1536]{2,1,0:T(8,128)(2,1)S(1)}, bf16[2,2048,1536]{1,2,0:T(8,128)(2,1)}, s32[2]{0:T(128)S(1)}, bf16[2,64,1536]{2,1,0:T(8,1...) while((s32[]{:T(128)}, bf16[2,64,1536]{2,1,0:T(8,128)(2,1)S(1)}, ...), condition=%wide.region_3.4_spmd.clone, body=%wide.region_0.3_spmd.clone.sunk | while | flops 828571648 | bytes 65302632 | solution.py:83
  284.7 11.9 %constant_dynamic-slice_fusion.5 = (bf16[1,2048,1536]{1,2,0:T(8,128)(2,1)}, bf16[1,2048,1536]{1,2,0:T(8,128)(2,1)}) fusion(bf16[2,2048,1536]{1,2,0:T(8,128)(2,1)} %get-tuple-element.212, s32[]{:T(128)} %get-tuple-element.200, bf16[2,2048,1536]{1,2,0:T(8,128)(2,1)} %get-tuple-element.209), kind=kLoop, calls=%fused_computation.20.clone.1 | loop fusion | bytes 25165828 | tf_op jit(solution)/shard_map/while/body/jit(dynamic_index_in_dim)/dynamic_slice | solution.py:83
  297.2 0.7 iota_compare_fusion.4
  298.2 5.0 fusion.182
  303.2 1.9 fusion.183
  305.1 5.1 fusion.184
  310.6 11.9 %constant_dynamic-slice_fusion.5 = (bf16[1,2048,1536]{1,2,0:T(8,128)(2,1)}, bf16[1,2048,1536]{1,2,0:T(8,128)(2,1)}) fusion(bf16[2,2048,1536]{1,2,0:T(8,128)(2,1)} %get-tuple-element.212, s32[]{:T(128)} %get-tuple-element.200, bf16[2,2048,1536]{1,2,0:T(8,128)(2,1)} %get-tuple-element.209), kind=kLoop, calls=%fused_computation.20.clone.1 | loop fusion | bytes 25165828 | tf_op jit(solution)/shard_map/while/body/jit(dynamic_index_in_dim)/dynamic_slice | solution.py:83
  323.1 0.7 iota_compare_fusion.4
  324.1 5.0 fusion.182
  329.1 1.9 fusion.183
  331.0 5.1 fusion.184
  336.6 5.0 convolution_bitcast_fusion
  341.6 0.8 fusion.37
  342.4 1.4 collective-permute-start
  343.9 1.5 collective-permute-start.1
  345.4 10.5 %reshape_reshape.6 = f32[18432,128]{1,0:T(8,128)} reshape(f32[1536,1536]{1,0:T(8,128)} %convolution_bitcast_fusion) | data formatting | bytes 18874368 | tf_op jit(solution)/shard_map/reshape;reshape | solution.py:34
  356.0 48.0 %gather_fusion = f32[23592,128]{1,0:T(8,128)} fusion(f32[18432,128]{1,0:T(8,128)} %reshape_reshape.6, s32[24576]{0:T(1024)S(1)} %pad_clamp_fusion), kind=kCustom, calls=%fused_computation | custom fusion | bytes 24252576 | tf_op jit(solution)/shard_map/jit(_take)/gather | solution.py:35
  404.3 22.9 %select_reduce_fusion = f32[23592]{0:T(1024)} fusion(f32[23592,128]{1,0:T(8,128)} %gather_fusion, s32[23592]{0:T(1024)S(1)} %copy-done.2, pred[23592]{0:T(1024)(128)(4,1)S(1)} %copy-done.4), kind=kLoop, calls=%fused_computation.25 | loop fusion | flops 12055512 | bytes 12291432 | tf_op jit(solution)/shard_map/reduce_sum | solution.py:38
  427.2 1.2 fusion.85
  428.6 1.3 fusion.101
  430.1 0.8 fusion.100
  431.0 0.8 fusion.84
  432.3 1.2 gather_fusion.1
  433.8 4.5 fusion.70
  438.6 60.1 %psum.30 = f32[476]{0:T(512)S(1)} all-reduce(f32[476]{0:T(512)S(1)} %select_reduce_fusion.1), channel_id=1, replica_groups=mesh['dp'=8,'seq'=32] {'seq'}, use_global_device_ids=true, to_apply=%region_39.40 | all-reduce | flops 476 | bytes 3808 | tf_op jit(solution)/shard_map/psum | solution.py:120
  498.7 27.1 %psum.31 = f32[476]{0:T(512)S(1)} all-reduce(f32[476]{0:T(512)S(1)} %psum.30), channel_id=1, replica_groups=mesh['dp'=8,'seq'=32] {'dp'}, use_global_device_ids=true, to_apply=%region_40.41 | all-reduce | flops 476 | bytes 3808 | tf_op jit(solution)/shard_map/psum | solution.py:120
  525.8 39.8 %all-reduce.3.cloned.1.call-done = f32[23592]{0:T(1024)} async-done(((f32[23592]{0:T(1024)}), f32[23592]{0:T(1024)}) %all-reduce.3.cloned.1.call-update) | async-done | bytes 94384 | tf_op jit(solution)/shard_map/psum | solution.py:120
  566.2 64.2 %all-reduce.5.cloned.1.call-done = f32[23592]{0:T(1024)} async-done(((f32[23592]{0:T(1024)}), f32[23592]{0:T(1024)}) %all-reduce.5.cloned.1.call-update) | async-done | bytes 94384 | tf_op jit(solution)/shard_map/psum | solution.py:120
  630.3 1.5 broadcast_multiply_fusion
  (217 shorter events, 5.1 us)
Async XLA Ops:
  7.2 127.1 %all-gather.3.cloned.1.call-start = ((), (), s32[]{:S(2)}) async-start(), calls=%async_computation | async-start | bytes 12976128 | tf_op jit(solution)/shard_map/all_gather | solution.py:63
  9.4 244.2 %all-gather.5.cloned.1.call-start = ((), (), s32[]{:S(2)}) async-start(), calls=%async_computation.1 | async-start | bytes 12976128 | tf_op jit(solution)/shard_map/all_gather | solution.py:62
  11.6 554.0 %all-reduce.3.cloned.1.call-start = ((), (), s32[]{:S(2)}) async-start(), calls=%async_computation.2 | async-start | bytes 196608 | tf_op jit(solution)/shard_map/psum | solution.py:120
  12.6 14.5 %collective-permute-start.2 = (bf16[2,15,1536]{2,1,0:T(8,128)(2,1)S(1)}, bf16[2,15,1536]{2,1,0:T(8,128)(2,1)S(1)}, u32[]{:S(2)}, u32[]{:S(2)}) collective-permute-start(bf16[2,15,1536]{2,1,0:T(8,128)(2,1)S(1)} %get-tuple-element.144), channel_id=1, source_target_pairs={{0,1},{1,2},{2,3},{3,4},{4,5},{5,6},{6,7},{7,8},{8,9},{9,10},{10,1... | collective-permute-start | bytes 276488 | tf_op jit(solution)/shard_map/ppermute | solution.py:18
  17.0 10.1 %collective-permute-start.3 = (bf16[2,15,1536]{2,1,0:T(8,128)(2,1)S(1)}, bf16[2,15,1536]{2,1,0:T(8,128)(2,1)S(1)}, u32[]{:S(2)}, u32[]{:S(2)}) collective-permute-start(bf16[2,15,1536]{2,1,0:T(8,128)(2,1)S(1)} %get-tuple-element.145), channel_id=1, source_target_pairs={{1,0},{2,1},{3,2},{4,3},{5,4},{6,5},{7,6},{8,7},{9,8},{10,9},{11,1... | collective-permute-start | bytes 276488 | tf_op jit(solution)/shard_map/ppermute | solution.py:19
  19.5 12.3 %copy-start.43 = (f32[1536]{0:T(1024)}, f32[1536]{0:T(1024)S(1)}, u32[]{:S(2)}) copy-start(f32[1536]{0:T(1024)S(1)} %get-tuple-element.112) | copy-start | bytes 18436
  165.4 119.3 %copy-start.1 = (bf16[2,64,1536]{2,1,0:T(8,128)(2,1)S(1)}, bf16[2,64,1536]{2,1,0:T(8,128)(2,1)}, u32[]{:S(2)}) copy-start(bf16[2,64,1536]{2,1,0:T(8,128)(2,1)} %param.12) | copy-start | bytes 1179652
  165.4 119.3 %copy-start.70 = (s32[2]{0:T(128)S(1)}, s32[2]{0:T(128)}, u32[]{:S(2)}) copy-start(s32[2]{0:T(128)} %param.16) | copy-start | bytes 28
  342.4 84.8 %collective-permute-start = (bf16[2,15,1536]{2,1,0:T(8,128)(2,1)S(1)}, bf16[2,15,1536]{2,1,0:T(8,128)(2,1)S(1)}, u32[]{:S(2)}, u32[]{:S(2)}) collective-permute-start(bf16[2,15,1536]{2,1,0:T(8,128)(2,1)S(1)} %get-tuple-element.146), channel_id=1, source_target_pairs={{0,1},{1,2},{2,3},{3,4},{4,5},{5,6},{6,7},{7,8},{8,9},{9,10},{10,1... | collective-permute-start | bytes 276488 | tf_op jit(solution)/shard_map/ppermute | solution.py:18
  343.9 84.6 %collective-permute-start.1 = (bf16[2,15,1536]{2,1,0:T(8,128)(2,1)S(1)}, bf16[2,15,1536]{2,1,0:T(8,128)(2,1)S(1)}, u32[]{:S(2)}, u32[]{:S(2)}) collective-permute-start(bf16[2,15,1536]{2,1,0:T(8,128)(2,1)S(1)} %get-tuple-element.147), channel_id=1, source_target_pairs={{1,0},{2,1},{3,2},{4,3},{5,4},{6,5},{7,6},{8,7},{9,8},{10,9},{11,1... | collective-permute-start | bytes 276488 | tf_op jit(solution)/shard_map/ppermute | solution.py:19
  356.0 48.0 %copy-start.2 = (s32[23592]{0:T(1024)S(1)}, s32[23592]{0:T(1024)}, u32[]{:S(2)}) copy-start(s32[23592]{0:T(1024)} %add_select_fusion.1) | copy-start | bytes 283108
  356.0 48.0 %copy-start.4 = (pred[23592]{0:T(1024)(128)(4,1)S(1)}, pred[23592]{0:T(1024)(128)(4,1)}, u32[]{:S(2)}) copy-start(pred[23592]{0:T(1024)(128)(4,1)} %get-tuple-element.138) | copy-start | bytes 70780
  403.9 23.3 %copy-start = (bf16[2,64,1536]{2,1,0:T(8,128)(2,1)S(1)}, bf16[2,64,1536]{2,1,0:T(8,128)(2,1)}, u32[]{:S(2)}) copy-start(bf16[2,64,1536]{2,1,0:T(8,128)(2,1)} %param.19) | copy-start | bytes 1179652
  403.9 28.3 %copy-start.67 = (s32[1024]{0:T(1024)S(1)}, s32[1024]{0:T(1024)}, u32[]{:S(2)}) copy-start(s32[1024]{0:T(1024)} %pad_clamp_fusion.1) | copy-start | bytes 12292
  403.9 29.5 %copy-start.6 = (f32[1536]{0:T(1024)S(1)}, f32[1536]{0:T(1024)}, u32[]{:S(2)}) copy-start(f32[1536]{0:T(1024)} %copy-done.5) | copy-start | bytes 18436
  403.9 29.5 %copy-start.8 = (f32[1536]{0:T(1024)S(1)}, f32[1536]{0:T(1024)}, u32[]{:S(2)}) copy-start(f32[1536]{0:T(1024)} %copy-done.7) | copy-start | bytes 18436
  404.0 29.5 %copy-start.10 = (f32[1536]{0:T(1024)S(1)}, f32[1536]{0:T(1024)}, u32[]{:S(2)}) copy-start(f32[1536]{0:T(1024)} %copy-done.9) | copy-start | bytes 18436
  404.0 29.5 %copy-start.12 = (f32[1536]{0:T(1024)S(1)}, f32[1536]{0:T(1024)}, u32[]{:S(2)}) copy-start(f32[1536]{0:T(1024)} %copy-done.11) | copy-start | bytes 18436
  404.0 29.5 %copy-start.14 = (f32[1536]{0:T(1024)S(1)}, f32[1536]{0:T(1024)}, u32[]{:S(2)}) copy-start(f32[1536]{0:T(1024)} %copy-done.13) | copy-start | bytes 18436
  404.0 29.5 %copy-start.16 = (f32[1536]{0:T(1024)S(1)}, f32[1536]{0:T(1024)}, u32[]{:S(2)}) copy-start(f32[1536]{0:T(1024)} %copy-done.15) | copy-start | bytes 18436
  404.0 29.5 %copy-start.18 = (f32[1536]{0:T(1024)S(1)}, f32[1536]{0:T(1024)}, u32[]{:S(2)}) copy-start(f32[1536]{0:T(1024)} %copy-done.17) | copy-start | bytes 18436
  404.0 29.5 %copy-start.20 = (f32[1536]{0:T(1024)S(1)}, f32[1536]{0:T(1024)}, u32[]{:S(2)}) copy-start(f32[1536]{0:T(1024)} %copy-done.19) | copy-start | bytes 18436
  404.0 29.5 %copy-start.22 = (f32[1536]{0:T(1024)S(1)}, f32[1536]{0:T(1024)}, u32[]{:S(2)}) copy-start(f32[1536]{0:T(1024)} %copy-done.21) | copy-start | bytes 18436
  404.0 29.5 %copy-start.24 = (f32[1536]{0:T(1024)S(1)}, f32[1536]{0:T(1024)}, u32[]{:S(2)}) copy-start(f32[1536]{0:T(1024)} %copy-done.23) | copy-start | bytes 18436
  404.0 29.5 %copy-start.26 = (f32[1536]{0:T(1024)S(1)}, f32[1536]{0:T(1024)}, u32[]{:S(2)}) copy-start(f32[1536]{0:T(1024)} %copy-done.25) | copy-start | bytes 18436
  404.0 29.5 %copy-start.28 = (f32[1536]{0:T(1024)S(1)}, f32[1536]{0:T(1024)}, u32[]{:S(2)}) copy-start(f32[1536]{0:T(1024)} %copy-done.27) | copy-start | bytes 18436
  404.1 29.5 %copy-start.30 = (f32[1536]{0:T(1024)S(1)}, f32[1536]{0:T(1024)}, u32[]{:S(2)}) copy-start(f32[1536]{0:T(1024)} %copy-done.29) | copy-start | bytes 18436
  404.1 29.5 %copy-start.32 = (f32[1536]{0:T(1024)S(1)}, f32[1536]{0:T(1024)}, u32[]{:S(2)}) copy-start(f32[1536]{0:T(1024)} %copy-done.31) | copy-start | bytes 18436
  404.1 29.5 %copy-start.34 = (f32[1536]{0:T(1024)S(1)}, f32[1536]{0:T(1024)}, u32[]{:S(2)}) copy-start(f32[1536]{0:T(1024)} %copy-done.33) | copy-start | bytes 18436
  404.1 29.5 %copy-start.36 = (f32[1536]{0:T(1024)S(1)}, f32[1536]{0:T(1024)}, u32[]{:S(2)}) copy-start(f32[1536]{0:T(1024)} %copy-done.35) | copy-start | bytes 18436
  404.1 29.5 %copy-start.38 = (f32[1536]{0:T(1024)S(1)}, f32[1536]{0:T(1024)}, u32[]{:S(2)}) copy-start(f32[1536]{0:T(1024)} %copy-done.37) | copy-start | bytes 18436
  404.1 29.5 %copy-start.40 = (f32[1536]{0:T(1024)S(1)}, f32[1536]{0:T(1024)}, u32[]{:S(2)}) copy-start(f32[1536]{0:T(1024)} %copy-done.39) | copy-start | bytes 18436
  404.1 29.5 %copy-start.42 = (f32[1536]{0:T(1024)S(1)}, f32[1536]{0:T(1024)}, u32[]{:S(2)}) copy-start(f32[1536]{0:T(1024)} %copy-done.41) | copy-start | bytes 18436
  404.1 29.5 %copy-start.44 = (f32[1536]{0:T(1024)S(1)}, f32[1536]{0:T(1024)}, u32[]{:S(2)}) copy-start(f32[1536]{0:T(1024)} %copy-done.43) | copy-start | bytes 18436
  404.1 29.5 %copy-start.46 = (f32[1536]{0:T(1024)S(1)}, f32[1536]{0:T(1024)}, u32[]{:S(2)}) copy-start(f32[1536]{0:T(1024)} %copy-done.45) | copy-start | bytes 18436
  404.1 29.5 %copy-start.48 = (f32[1536]{0:T(1024)S(1)}, f32[1536]{0:T(1024)}, u32[]{:S(2)}) copy-start(f32[1536]{0:T(1024)} %copy-done.47) | copy-start | bytes 18436
  404.2 29.5 %copy-start.50 = (f32[1536]{0:T(1024)S(1)}, f32[1536]{0:T(1024)}, u32[]{:S(2)}) copy-start(f32[1536]{0:T(1024)} %copy-done.49) | copy-start | bytes 18436
  404.2 29.5 %copy-start.52 = (f32[1536]{0:T(1024)S(1)}, f32[1536]{0:T(1024)}, u32[]{:S(2)}) copy-start(f32[1536]{0:T(1024)} %copy-done.51) | copy-start | bytes 18436
  404.2 29.5 %copy-start.54 = (f32[1536]{0:T(1024)S(1)}, f32[1536]{0:T(1024)}, u32[]{:S(2)}) copy-start(f32[1536]{0:T(1024)} %copy-done.53) | copy-start | bytes 18436
  404.2 29.5 %copy-start.56 = (f32[1536]{0:T(1024)S(1)}, f32[1536]{0:T(1024)}, u32[]{:S(2)}) copy-start(f32[1536]{0:T(1024)} %copy-done.55) | copy-start | bytes 18436
  404.2 29.5 %copy-start.58 = (f32[1536]{0:T(1024)S(1)}, f32[1536]{0:T(1024)}, u32[]{:S(2)}) copy-start(f32[1536]{0:T(1024)} %copy-done.57) | copy-start | bytes 18436
  404.2 29.5 %copy-start.60 = (f32[1536]{0:T(1024)S(1)}, f32[1536]{0:T(1024)}, u32[]{:S(2)}) copy-start(f32[1536]{0:T(1024)} %copy-done.59) | copy-start | bytes 18436
  404.2 29.5 %copy-start.62 = (f32[1536]{0:T(1024)S(1)}, f32[1536]{0:T(1024)}, u32[]{:S(2)}) copy-start(f32[1536]{0:T(1024)} %copy-done.61) | copy-start | bytes 18436
  404.2 29.5 %copy-start.64 = (f32[1536]{0:T(1024)S(1)}, f32[1536]{0:T(1024)}, u32[]{:S(2)}) copy-start(f32[1536]{0:T(1024)} %copy-done.63) | copy-start | bytes 18436
  404.2 29.5 %copy-start.66 = (f32[1536]{0:T(1024)S(1)}, f32[1536]{0:T(1024)}, u32[]{:S(2)}) copy-start(f32[1536]{0:T(1024)} %copy-done.65) | copy-start | bytes 18436
  404.2 34.0 %copy-start.68 = (s32[476]{0:T(512)S(1)}, s32[476]{0:T(512)}, u32[]{:S(2)}) copy-start(s32[476]{0:T(512)} %add_select_fusion.3) | copy-start | bytes 5716
  404.3 34.0 %copy-start.69 = (pred[476]{0:T(512)(128)(4,1)S(1)}, pred[476]{0:T(512)(128)(4,1)}, u32[]{:S(2)}) copy-start(pred[476]{0:T(512)(128)(4,1)} %get-tuple-element.136) | copy-start | bytes 1432
  427.2 203.2 %all-reduce.5.cloned.1.call-start = ((), (), s32[]{:S(2)}) async-start(), calls=%async_computation.3 | async-start | bytes 196608 | tf_op jit(solution)/shard_map/psum | solution.py:120
  (35 other events, 387.6 us)
Sparse Core Ops, SparseCore 0:
  11.2 123.0 all-gather.2
  136.8 116.7 all-gather.4
  427.3 138.2 all-reduce.2
  567.8 62.5 all-reduce.4
